TPU v7x, 256 devices: a whole 4x4x8 slice. The times are simulated.
256 devices in a mesh: dp: 32 (over x, y, core), tensor: 8 (over z).
Axes of the slice: x: 4, y: 4, z: 8, core: 2. Of those that a mesh axis runs over, the one named last changes fastest.
Arguments:
- hidden_states: bfloat16 [24576, 4096], P('dp', 'tensor')
- neighbour_ids: int32 [384, 2], P('dp'), may hold values from 0 to 511, as said below
- database: bfloat16 [512, 128, 896], P('dp')
- w_up: bfloat16 [896, 3584], P(None, 'tensor'), may hold values from -0.1875 to 0.1875
- w_down: bfloat16 [3584, 896], P('tensor'), may hold values from -0.09375 to 0.09375
- w_query: bfloat16 [4096, 4096], P(None, 'tensor'), may hold values from -0.09375 to 0.09375
- w_key: bfloat16 [896, 4096], P(None, 'tensor'), may hold values from -0.1875 to 0.1875
- w_value: bfloat16 [896, 4096], P(None, 'tensor'), may hold values from -0.1875 to 0.1875
Outputs:
- attended: bfloat16 [24576, 4096], P('dp', 'tensor')
Inputs may be any that keep to these rules, and one draw needn't show every extreme that they name: `neighbour_ids`: block ids are grouped by owner: index s of dp holds blocks s * 16 to (s + 1) * 16 - 1. Among the 24 ids of one sequence, no owner's blocks are named more than 2 times; one owner, the same for every sequence, is named exactly 2 times by each.
All inputs are finite; a program needn't handle non-finite values.
Results may differ from a plain program's by a relative error of at most 0.02.
Values may be sent and summed in bfloat16 or wider, within the bound.
No kernel may reach another device: no remote copies, remote signals or barrier semaphores. Data moves between devices by JAX's collectives and lax.ppermute only.
A program may use at most 128 MiB of HBM per device.

v0:
```python
import math
import jax
import jax.numpy as jnp
from jax import lax
from jax.sharding import PartitionSpec as P

HD = 128
SPAN = 64
KN = 2
NTOK = 128
EPSILON = 1e-06
LOGIT_SCALE = 3.0


def head_norm(projected):
    shaped = projected.reshape(projected.shape[0], -1, HD)
    scaled = shaped * lax.rsqrt(jnp.mean(shaped * shaped, axis=-1, keepdims=True) + EPSILON)
    return scaled.astype(jnp.bfloat16)


def attend(queries, keys, values):
    seq_rows = queries.shape[0]
    heads_here = queries.shape[1]
    span_count = seq_rows // SPAN
    shifted = jnp.concatenate(
        [queries[SPAN - 1 :], jnp.zeros((SPAN - 1, heads_here, HD), jnp.bfloat16)], axis=0
    )
    windows = shifted.reshape(span_count, SPAN, heads_here, HD)
    key_blocks = keys.reshape(span_count, KN * NTOK, heads_here, HD)
    value_blocks = values.reshape(span_count, KN * NTOK, heads_here, HD)
    scores = jnp.einsum("cqhd,ckhd->chqk", windows, key_blocks, preferred_element_type=jnp.float32)
    scores = scores * (LOGIT_SCALE / math.sqrt(HD))
    expo = jnp.exp(scores)
    weights = (expo / jnp.sum(expo, axis=-1, keepdims=True)).astype(jnp.bfloat16)
    mixed = jnp.einsum("chqk,ckhd->cqhd", weights, value_blocks, preferred_element_type=jnp.float32)
    mixed = mixed.astype(jnp.bfloat16).reshape(seq_rows, heads_here * HD)
    leading = jnp.zeros((SPAN - 1, heads_here * HD), jnp.bfloat16)
    return jnp.concatenate([leading, mixed[: seq_rows - SPAN + 1]], axis=0)


def shards(hidden_states, neighbour_ids, database, w_up, w_down, w_query, w_key, w_value):
    dp_count = lax.axis_size("dp")
    tensor_count = lax.axis_size("tensor")
    shard_blocks = database.shape[0]
    block_tokens = database.shape[1]
    enc_width = database.shape[2]
    flat_ids = neighbour_ids.reshape(-1)
    request_count = flat_ids.shape[0]
    capacity = max(2, (request_count + dp_count - 1) // dp_count + 1)
    owners = flat_ids // shard_blocks
    local_rows = flat_ids % shard_blocks
    owner_match = (owners[:, None] == jnp.arange(dp_count, dtype=jnp.int32)[None, :]).astype(
        jnp.int32
    )
    positions = jnp.arange(request_count, dtype=jnp.int32)
    earlier = (positions[:, None] > positions[None, :]).astype(jnp.int32)
    ranks = jnp.sum(jnp.dot(earlier, owner_match) * owner_match, axis=1)
    slots = owners * capacity + ranks
    slot_match = slots[None, :] == jnp.arange(dp_count * capacity, dtype=jnp.int32)[:, None]
    requests = jnp.sum(jnp.where(slot_match, local_rows[None, :], 0), axis=1)
    requests = requests.reshape(dp_count, capacity)
    replies = lax.all_to_all(
        database[lax.all_to_all(requests, "dp", split_axis=0, concat_axis=0, tiled=True)],
        "dp",
        split_axis=0,
        concat_axis=0,
        tiled=True,
    )
    raw_blocks = replies.reshape(dp_count * capacity, block_tokens, enc_width)[slots]
    raw_float = raw_blocks.astype(jnp.float32)
    normed = (
        raw_float * lax.rsqrt(jnp.mean(raw_float * raw_float, axis=-1, keepdims=True) + EPSILON)
    ).astype(jnp.bfloat16)
    own_blocks = request_count // tensor_count
    inner = jnp.einsum("bte,ef->btf", normed, w_up, preferred_element_type=jnp.float32)
    active = jax.nn.gelu(inner).astype(jnp.bfloat16)
    summed = lax.psum_scatter(
        jnp.einsum("btf,fe->bte", active, w_down, preferred_element_type=jnp.float32).astype(
            jnp.bfloat16
        ),
        "tensor",
        scatter_dimension=0,
        tiled=True,
    ).astype(jnp.float32)
    raw_own = lax.dynamic_slice_in_dim(
        raw_float, lax.axis_index("tensor") * own_blocks, own_blocks, 0
    )
    encoded_own = (raw_own + summed).astype(jnp.bfloat16)
    encoded = lax.all_gather(encoded_own, "tensor", axis=0, tiled=True)
    projected = jnp.dot(
        lax.all_gather(hidden_states, "tensor", axis=1, tiled=True),
        w_query,
        preferred_element_type=jnp.float32,
    )
    queries = head_norm(projected)
    flat_encoded = encoded.reshape(-1, enc_width)
    keys = head_norm(jnp.dot(flat_encoded, w_key, preferred_element_type=jnp.float32))
    values = jnp.dot(flat_encoded, w_value, preferred_element_type=jnp.float32).astype(jnp.bfloat16)
    values = values.reshape(flat_encoded.shape[0], -1, HD)
    return attend(queries, keys, values)


def solution(mesh):
    in_specs = (
        P("dp", "tensor"),
        P("dp", None),
        P("dp", None, None),
        P(None, "tensor"),
        P("tensor", None),
        P(None, "tensor"),
        P(None, "tensor"),
        P(None, "tensor"),
    )
    out_specs = P("dp", "tensor")
    return jax.shard_map(shards, mesh=mesh, in_specs=in_specs, out_specs=out_specs, check_vma=False)
```

profile of v0, /device:TPU:1, one launch (start us, length us, event | category | flops | bytes accessed | tf_op | source)
XLA Modules:
  0.0 541.9 jit_solution(13727991307017011752)
XLA Ops:
  6.5 0.0 copy-start
  6.5 0.8 copy.37
  7.4 0.1 reshape.233
  7.5 0.3 fusion.29
  7.8 0.1 select_reduce_fusion
  7.9 0.1 all_to_all.11
  8.0 15.3 %all_to_all.17 = s32[32,1,2]{2,1,0:T(1,128)S(1)} all-to-all(s32[32,1,2]{2,1,0:T(1,128)S(1)} %bitcast.50), channel_id=1, replica_groups=mesh['dp'=32,'tensor'=8] {'dp'}, dimensions={0} | all-to-all | bytes 512 | tf_op jit(solution)/shard_map/all_to_all | solution.py:63
  23.4 0.1 copy.39
  23.4 0.1 copy.40
  23.5 0.1 reshape.243
  23.7 10.0 %gather_fusion = bf16[64,128,896]{2,1,0:T(8,128)(2,1)} fusion(bf16[16,128,896]{2,1,0:T(8,128)(2,1)} %param.10, s32[1024]{0:T(1024)S(1)} %pad_clamp_fusion.1), kind=kCustom, calls=%fused_computation | custom fusion | bytes 29360384 | tf_op jit(solution)/shard_map/gather | solution.py:63
  33.7 5.4 %all-to-all-start.1 = ((bf16[32,2,128,896]{3,2,1,0:T(8,128)(2,1)}), bf16[32,2,128,896]{3,2,1,0:T(8,128)(2,1)}, u32[]{:S(2)}, u32[]{:S(2)}) async-start(bf16[32,2,128,896]{3,2,1,0:T(8,128)(2,1)} %bitcast.42), calls=%async_computation.1 | async-start | bytes 29360128 | tf_op jit(solution)/shard_map/all_to_all | solution.py:62
  39.1 0.0 reduce-scatter.2.cloned.1.call-start
  39.2 0.1 reshape.235
  39.3 202.2 %all-to-all-done.1 = bf16[32,2,128,896]{3,2,1,0:T(8,128)(2,1)} async-done(((bf16[32,2,128,896]{3,2,1,0:T(8,128)(2,1)}), bf16[32,2,128,896]{3,2,1,0:T(8,128)(2,1)}, u32[]{:S(2)}, u32[]{:S(2)}) %all-to-all-start.1) | async-done | bytes 14680096 | tf_op jit(solution)/shard_map/all_to_all | solution.py:62
  241.5 9.1 %gather_fusion.1 = bf16[24,128,896]{2,1,0:T(8,128)(2,1)} fusion(bf16[64,128,896]{2,1,0:T(8,128)(2,1)} %bitcast.3, s32[1024]{0:T(1024)S(1)} %pad_clamp_fusion), kind=kCustom, calls=%fused_computation.1 | custom fusion | bytes 11010144 | tf_op jit(solution)/shard_map/gather | solution.py:69
  250.5 0.0 copy-start.4
  250.5 0.0 copy-start.5
  250.5 3.8 multiply_reduce_fusion
  254.4 0.0 copy-done.4
  254.4 0.0 copy-done.5
  254.4 10.4 %convolution_convert_fusion.1 = bf16[24,128,896]{2,1,0:T(8,128)(2,1)} fusion(f32[24,128]{1,0:T(8,128)S(1)} %add_rsqrt_fusion.2, bf16[24,128,896]{2,1,0:T(8,128)(2,1)} %gather_fusion.1, bf16[448,896]{1,0:T(8,128)(2,1)S(1)} %copy-done.4, bf16[896,448]{0,1:T(8,128)(2,1)S(1)} %copy-done.5), kind=kOutput, calls=%fused_computation.19 | convolution fusion | flops 4955897856 | bytes 12627968 | tf_op jit(solution)/shard_map/btf,fe->bte/dot_general | solution.py:78
  264.8 0.0 reduce-scatter.2.cloned.1.call-update
  264.9 0.0 all-gather.5.cloned.1.call-start
  264.9 0.7 all-gather.5.cloned.1.call-update
  265.6 0.2 all-gather.3.cloned.1.call-start
  265.9 0.0 copy-start.2
  265.9 8.2 %convert_element_type.38 = f32[24,128,896]{2,1,0:T(8,128)} convert(bf16[24,128,896]{2,1,0:T(8,128)(2,1)} %gather_fusion.1) | non-fusion elementwise | flops 2752512 | bytes 16515072 | tf_op jit(solution)/shard_map/convert_element_type | solution.py:70
  274.0 90.7 %reduce-scatter.2.cloned.1.call-done = bf16[3,128,896]{2,1,0:T(8,128)(2,1)} async-done(((bf16[24,128,896]{2,1,0:T(8,128)(2,1)}), bf16[3,128,896]{2,1,0:T(8,128)(2,1)}) %reduce-scatter.2.cloned.1.call-update) | async-done | bytes 688144 | tf_op jit(solution)/shard_map/reduce_scatter | solution.py:77
  364.8 2.5 add_convert_fusion
  367.3 0.0 all-gather.3.cloned.1.call-update
  367.3 0.0 copy-done.2
  367.3 0.6 copy.48
  367.9 71.6 %all-gather.5.cloned.1.call-done = bf16[768,4096]{1,0:T(8,128)(2,1)} async-done(((bf16[768,512]{1,0:T(8,128)(2,1)}), bf16[768,4096]{1,0:T(8,128)(2,1)}) %all-gather.5.cloned.1.call-update) | async-done | bytes 6291472 | tf_op jit(solution)/shard_map/all_gather | solution.py:91
  439.5 7.1 %multiply_reduce_fusion.2 = (f32[768,4]{0,1:T(4,128)S(1)}, f32[768,512]{0,1:T(8,128)S(1)}) fusion(bf16[768,4096]{1,0:T(8,128)(2,1)} %all-gather.5.cloned.1.call-done, bf16[4096,512]{1,0:T(8,128)(2,1)} %param.13), kind=kOutput, calls=%fused_computation.33 | convolution fusion | flops 3222008832 | bytes 12070912 | tf_op jit(solution)/shard_map/dot_general | solution.py:90
  446.7 0.5 slice.12
  447.2 1.6 copy.49
  448.8 0.1 slice.13
  448.9 1.8 multiply_convert_fusion.3
  450.7 0.1 concatenate.6
  450.7 56.3 %all-gather.3.cloned.1.call-done = bf16[24,128,896]{2,1,0:T(8,128)(2,1)} async-done(((bf16[3,128,896]{2,1,0:T(8,128)(2,1)}), bf16[24,128,896]{2,1,0:T(8,128)(2,1)}) %all-gather.3.cloned.1.call-update) | async-done | bytes 5505040 | tf_op jit(solution)/shard_map/all_gather | solution.py:89
  507.0 0.0 copy-start.3
  507.0 8.6 %multiply_reduce_fusion.1 = (f32[3072,4]{0,1:T(4,128)S(1)}, f32[3072,4,128]{2,0,1:T(8,128)}) fusion(bf16[3072,896,1]{1,0,2:T(8,128)(2,1)} %bitcast.51, bf16[4,128,896]{2,1,0:T(8,128)(2,1)S(1)} %bitcast.49), kind=kOutput, calls=%fused_computation.6 | convolution fusion | flops 2821705728 | bytes 12763136 | tf_op jit(solution)/shard_map/dot_general | solution.py:97
  515.6 0.0 copy-done
  515.6 0.0 copy-done.3
  515.6 4.8 convolution_convert_fusion
  520.4 5.6 %reshape_reshape.3 = bf16[12,256,4,128]{3,2,1,0:T(4,128)(2,1)} reshape(bf16[3072,512]{1,0:T(8,128)(2,1)} %convolution_convert_fusion) | data formatting | bytes 6291456 | tf_op jit(solution)/shard_map/reshape;reshape | solution.py:30
  526.0 4.4 multiply_convert_fusion.1
  530.4 0.0 copy-start.1
  530.4 1.3 fusion.15
  531.7 0.6 copy-done.1
  532.3 1.2 fusion.26
  533.5 0.6 copy.47
  534.1 0.1 copy.66
  534.3 1.1 concatenate.7
  (10 shorter events, 0.1 us)
Async XLA Ops:
  6.5 509.1 %copy-start = (bf16[896,512]{1,0:T(8,128)(2,1)S(1)}, bf16[896,512]{1,0:T(8,128)(2,1)}, u32[]{:S(2)}) copy-start(bf16[896,512]{1,0:T(8,128)(2,1)} %param.15) | copy-start | bytes 2752516
  33.7 207.8 %all-to-all-start.1 = ((bf16[32,2,128,896]{3,2,1,0:T(8,128)(2,1)}), bf16[32,2,128,896]{3,2,1,0:T(8,128)(2,1)}, u32[]{:S(2)}, u32[]{:S(2)}) async-start(bf16[32,2,128,896]{3,2,1,0:T(8,128)(2,1)} %bitcast.42), calls=%async_computation.1 | async-start | bytes 29360128 | tf_op jit(solution)/shard_map/all_to_all | solution.py:62
  39.1 325.6 %reduce-scatter.2.cloned.1.call-start = ((), (), s32[]{:S(2)}) async-start(), calls=%async_computation.3 | async-start | bytes 6193152 | tf_op jit(solution)/shard_map/reduce_scatter | solution.py:77
  250.5 3.8 copy-start.4
  250.5 3.9 copy-start.5
  264.9 174.7 %all-gather.5.cloned.1.call-start = ((), (), s32[]{:S(2)}) async-start(), calls=%async_computation.5 | async-start | bytes 7077888 | tf_op jit(solution)/shard_map/all_gather | solution.py:91
  265.6 241.4 %all-gather.3.cloned.1.call-start = ((), (), s32[]{:S(2)}) async-start(), calls=%async_computation.4 | async-start | bytes 6193152 | tf_op jit(solution)/shard_map/all_gather | solution.py:89
  265.9 101.5 %copy-start.2 = (bf16[896,512]{1,0:T(8,128)(2,1)S(1)}, bf16[896,512]{1,0:T(8,128)(2,1)}, u32[]{:S(2)}) copy-start(bf16[896,512]{1,0:T(8,128)(2,1)} %param.14) | copy-start | bytes 2752516
  507.0 8.6 %copy-start.3 = (bf16[24,128,896]{2,1,0:T(8,128)(2,1)S(1)}, bf16[24,128,896]{2,1,0:T(8,128)(2,1)}, u32[]{:S(2)}) copy-start(bf16[24,128,896]{2,1,0:T(8,128)(2,1)} %all-gather.3.cloned.1.call-done) | copy-start | bytes 16515076
  530.4 1.9 copy-start.1
Sparse Core Ops, SparseCore 0:
  265.0 99.7 reduce-scatter.1
  366.6 72.9 all-gather.4
  441.3 65.6 all-gather.2
where the time goes:
time: 542 us
  waiting for transfers between devices  422 us (78%)
  matrix products  33.7 us (6%)
  local copies, waits for them, and re-layouts  31.3 us (6%)
  other arithmetic  20.9 us (4%)
  blocking collectives  15.3 us (3%)
  between operations  13.3 us (2%)
  starting transfers between devices  5.75 us (1%)
    all_to_all x1, waiting for transfers between devices, shards(): lax.all_to_all(database[lax.all_to_all(requests, 'dp', split_axis=0, conc...  202 us
    reduce_scatter x1, waiting for transfers between devices, shards(): lax.psum_scatter(jnp.einsum('btf,fe->bte', active, w_down, preferred_elem...  90.7 us
    all_gather x1, waiting for transfers between devices, shards(): lax.all_gather(hidden_states, 'tensor', axis=1, tiled=True)  71.6 us
    all_gather x1, waiting for transfers between devices, shards(): encoded = lax.all_gather(encoded_own, 'tensor', axis=0, tiled=True)  56.3 us
    all_to_all x1, blocking collectives, shards(): lax.all_to_all(requests, 'dp', split_axis=0, concat_axis=0, tiled=True)  15.3 us
  transfers between devices with their start and end apart: 4, of which 4 were waited for; matrix products, arithmetic and copies ran while one was open for 4% of the time, Pallas kernels for 0%

commit v1 on v0

--- a/solution.py
+++ b/solution.py
@@ -86,7 +86,11 @@
         raw_float, lax.axis_index("tensor") * own_blocks, own_blocks, 0
     )
     encoded_own = (raw_own + summed).astype(jnp.bfloat16)
-    encoded = lax.all_gather(encoded_own, "tensor", axis=0, tiled=True)
+    length = lax.axis_size("tensor")
+    repeats = [length if d == 0 else 1 for d in range(encoded_own.ndim)]
+    encoded = lax.all_to_all(
+        jnp.tile(encoded_own, repeats), "tensor", split_axis=0, concat_axis=0, tiled=True
+    )
     projected = jnp.dot(
         lax.all_gather(hidden_states, "tensor", axis=1, tiled=True),
         w_query,

time: 542 us -> 604 us (1.11)
  waiting for transfers between devices: 422 us -> 473 us
    all_gather x1, waiting for transfers between devices: 71.6 us -> 179 us  [shards(): lax.all_gather(hidden_states, 'tensor', axis=1, tiled=True)]
    all_gather x1 -> x0, waiting for transfers between devices: 56.3 us -> none  [shards(): encoded = lax.all_gather(encoded_own, 'tensor', axis=0, tiled=True)]
  transfers between devices with their start and end apart: 4 -> 4, of which waited for: 4 -> 3; matrix products, arithmetic and copies ran while one was open for 4% -> 4% of each run, Pallas kernels for 0% -> 0%
where the time goes in v1:
time: 604 us; the launch traced here: 603 us
  waiting for transfers between devices  473 us (78%)
  matrix products  36 us (6%)
  local copies, waits for them, and re-layouts  34.5 us (6%)
  other arithmetic  20 us (3%)
  blocking collectives  15.3 us (3%)
  between operations  13.6 us (2%)
  starting transfers between devices  10.5 us (2%)
    all_to_all x1, waiting for transfers between devices, shards(): lax.all_to_all(database[lax.all_to_all(requests, 'dp', split_axis=0, conc...  202 us
    all_gather x1, waiting for transfers between devices, shards(): lax.all_gather(hidden_states, 'tensor', axis=1, tiled=True)  179 us
    reduce_scatter x1, waiting for transfers between devices, shards(): lax.psum_scatter(jnp.einsum('btf,fe->bte', active, w_down, preferred_elem...  91.1 us
    all_to_all x1, blocking collectives, shards(): lax.all_to_all(requests, 'dp', split_axis=0, concat_axis=0, tiled=True)  15.3 us
  transfers between devices with their start and end apart: 4, of which 3 were waited for; matrix products, arithmetic and copies ran while one was open for 4% of the time, Pallas kernels for 0%

profile of v1, /device:TPU:1, one launch (start us, length us, event | category | flops | bytes accessed | tf_op | source)
XLA Modules:
  0.0 603.0 jit_solution(15111456077777251626)
XLA Ops:
  6.5 0.0 copy-start
  6.5 0.8 copy.37
  7.4 0.1 reshape.237
  7.5 0.3 fusion.29
  7.8 0.1 select_reduce_fusion
  7.9 0.1 all_to_all.14
  8.0 15.3 %all_to_all.22 = s32[32,1,2]{2,1,0:T(1,128)S(1)} all-to-all(s32[32,1,2]{2,1,0:T(1,128)S(1)} %bitcast.52), channel_id=1, replica_groups=mesh['dp'=32,'tensor'=8] {'dp'}, dimensions={0} | all-to-all | bytes 512 | tf_op jit(solution)/shard_map/all_to_all | solution.py:63
  23.4 0.1 copy.39
  23.4 0.1 copy.40
  23.5 0.1 reshape.247
  23.7 10.0 %gather_fusion = bf16[64,128,896]{2,1,0:T(8,128)(2,1)} fusion(bf16[16,128,896]{2,1,0:T(8,128)(2,1)} %param.10, s32[1024]{0:T(1024)S(1)} %pad_clamp_fusion.1), kind=kCustom, calls=%fused_computation | custom fusion | bytes 29360384 | tf_op jit(solution)/shard_map/gather | solution.py:63
  33.7 5.4 all-to-all-start.1
  39.1 0.0 reduce-scatter.2.cloned.1.call-start
  39.2 0.1 reshape.239
  39.3 202.2 %all-to-all-done.1 = bf16[32,2,128,896]{3,2,1,0:T(8,128)(2,1)} async-done(((bf16[32,2,128,896]{3,2,1,0:T(8,128)(2,1)}), bf16[32,2,128,896]{3,2,1,0:T(8,128)(2,1)}, u32[]{:S(2)}, u32[]{:S(2)}) %all-to-all-start.1) | async-done | bytes 14680096 | tf_op jit(solution)/shard_map/all_to_all | solution.py:62
  241.5 9.1 %gather_fusion.1 = bf16[24,128,896]{2,1,0:T(8,128)(2,1)} fusion(bf16[64,128,896]{2,1,0:T(8,128)(2,1)} %bitcast.3, s32[1024]{0:T(1024)S(1)} %pad_clamp_fusion), kind=kCustom, calls=%fused_computation.1 | custom fusion | bytes 11010144 | tf_op jit(solution)/shard_map/gather | solution.py:69
  250.6 0.0 copy-start.3
  250.6 0.0 copy-start.4
  250.6 3.8 multiply_reduce_fusion
  254.4 0.0 copy-done.3
  254.4 0.0 copy-done.4
  254.4 10.4 %convolution_convert_fusion.1 = bf16[24,128,896]{2,1,0:T(8,128)(2,1)} fusion(f32[24,128]{1,0:T(8,128)S(1)} %add_rsqrt_fusion.2, bf16[24,128,896]{2,1,0:T(8,128)(2,1)} %gather_fusion.1, bf16[448,896]{1,0:T(8,128)(2,1)S(1)} %copy-done.3, bf16[896,448]{0,1:T(8,128)(2,1)S(1)} %copy-done.4), kind=kOutput, calls=%fused_computation.19 | convolution fusion | flops 4955897856 | bytes 12627968 | tf_op jit(solution)/shard_map/btf,fe->bte/dot_general | solution.py:78
  264.8 0.0 reduce-scatter.2.cloned.1.call-update
  264.9 0.0 all-gather.2.cloned.1.call-start
  264.9 0.7 all-gather.2.cloned.1.call-update
  265.6 8.1 %convert_element_type.38 = f32[24,128,896]{2,1,0:T(8,128)} convert(bf16[24,128,896]{2,1,0:T(8,128)(2,1)} %gather_fusion.1) | non-fusion elementwise | flops 2752512 | bytes 16515072 | tf_op jit(solution)/shard_map/convert_element_type | solution.py:70
  273.7 91.1 %reduce-scatter.2.cloned.1.call-done = bf16[3,128,896]{2,1,0:T(8,128)(2,1)} async-done(((bf16[24,128,896]{2,1,0:T(8,128)(2,1)}), bf16[3,128,896]{2,1,0:T(8,128)(2,1)}) %reduce-scatter.2.cloned.1.call-update) | async-done | bytes 688144 | tf_op jit(solution)/shard_map/reduce_scatter | solution.py:77
  364.8 1.7 add_convert_fusion
  366.4 3.2 tile.4
  369.6 0.0 copy-start.2
  369.6 5.0 all-to-all-start.2
  374.6 0.0 copy-done.2
  374.6 0.6 copy.48
  375.2 179.1 %all-gather.2.cloned.1.call-done = bf16[768,4096]{1,0:T(8,128)(2,1)} async-done(((bf16[768,512]{1,0:T(8,128)(2,1)}), bf16[768,4096]{1,0:T(8,128)(2,1)}) %all-gather.2.cloned.1.call-update) | async-done | bytes 6291472 | tf_op jit(solution)/shard_map/all_gather | solution.py:95
  554.3 7.1 %multiply_reduce_fusion.2 = (f32[768,4]{0,1:T(4,128)S(1)}, f32[768,512]{0,1:T(8,128)S(1)}) fusion(bf16[768,4096]{1,0:T(8,128)(2,1)} %all-gather.2.cloned.1.call-done, bf16[4096,512]{1,0:T(8,128)(2,1)} %param.13), kind=kOutput, calls=%fused_computation.33 | convolution fusion | flops 3222008832 | bytes 12070912 | tf_op jit(solution)/shard_map/dot_general | solution.py:94
  561.5 0.5 slice.12
  561.9 1.6 copy.49
  563.6 0.1 slice.13
  563.7 1.8 multiply_convert_fusion.3
  565.5 0.1 concatenate.6
  565.5 0.0 all-to-all-done.2
  565.6 8.2 %multiply_reduce_fusion.1 = (f32[3072,4]{0,1:T(4,128)S(1)}, f32[3072,4,128]{2,0,1:T(8,128)}) fusion(bf16[3072,896,1]{1,0,2:T(8,128)(2,1)} %bitcast.12, bf16[4,128,896]{2,1,0:T(8,128)(2,1)S(1)} %bitcast.51), kind=kOutput, calls=%fused_computation.6 | convolution fusion | flops 2821705728 | bytes 12763136 | tf_op jit(solution)/shard_map/dot_general | solution.py:101
  573.8 0.0 copy-done
  573.8 7.4 %convolution_convert_fusion = bf16[3072,512]{1,0:T(8,128)(2,1)} fusion(bf16[3072,896]{1,0:T(8,128)(2,1)} %bitcast.9, bf16[896,512]{1,0:T(8,128)(2,1)S(1)} %copy-done), kind=kOutput, calls=%fused_computation.18 | convolution fusion | flops 2820145152 | bytes 9568256 | tf_op jit(solution)/shard_map/dot_general | solution.py:102
  581.2 5.5 reshape_reshape.3
  586.7 4.4 multiply_convert_fusion.1
  591.2 0.0 copy-start.1
  591.2 1.3 fusion.15
  592.5 0.6 copy-done.1
  593.1 1.2 fusion.26
  594.3 0.6 copy.47
  594.9 0.1 copy.66
  595.1 1.1 concatenate.7
  (10 shorter events, 0.1 us)
Async XLA Ops:
  6.5 567.2 %copy-start = (bf16[896,512]{1,0:T(8,128)(2,1)S(1)}, bf16[896,512]{1,0:T(8,128)(2,1)}, u32[]{:S(2)}) copy-start(bf16[896,512]{1,0:T(8,128)(2,1)} %param.15) | copy-start | bytes 2752516
  33.7 207.8 %all-to-all-start.1 = ((bf16[32,2,128,896]{3,2,1,0:T(8,128)(2,1)}), bf16[32,2,128,896]{3,2,1,0:T(8,128)(2,1)}, u32[]{:S(2)}, u32[]{:S(2)}) async-start(bf16[32,2,128,896]{3,2,1,0:T(8,128)(2,1)} %bitcast.43), calls=%async_computation.1 | async-start | bytes 29360128 | tf_op jit(solution)/shard_map/all_to_all | solution.py:62
  39.1 325.6 %reduce-scatter.2.cloned.1.call-start = ((), (), s32[]{:S(2)}) async-start(), calls=%async_computation.4 | async-start | bytes 6193152 | tf_op jit(solution)/shard_map/reduce_scatter | solution.py:77
  250.6 3.8 copy-start.3
  250.6 3.9 copy-start.4
  264.9 289.5 %all-gather.2.cloned.1.call-start = ((), (), s32[]{:S(2)}) async-start(), calls=%async_computation.5 | async-start | bytes 7077888 | tf_op jit(solution)/shard_map/all_gather | solution.py:95
  369.6 5.0 copy-start.2
  369.6 195.9 %all-to-all-start.2 = ((bf16[24,128,896]{2,1,0:T(8,128)(2,1)}), bf16[24,128,896]{2,1,0:T(8,128)(2,1)}, u32[]{:S(2)}, u32[]{:S(2)}) async-start(bf16[24,128,896]{2,1,0:T(8,128)(2,1)} %bitcast.44), calls=%async_computation.3 | async-start | bytes 11010048 | tf_op jit(solution)/shard_map/all_to_all | solution.py:91
  591.2 1.9 copy-start.1
Sparse Core Ops, SparseCore 0:
  265.0 99.7 reduce-scatter.1
  366.6 187.7 all-gather.1
